TPU v7x, 32 devices: a whole 2x2x4 slice. The times are simulated.
32 devices in a mesh: dp: 8 (over y, x, core), expert: 4 (over z).
Axes of the slice: x: 2, y: 2, z: 4, core: 2. Of those that a mesh axis runs over, the one named last changes fastest.
Arguments:
- tokens: bfloat16 [4096, 1024], P(('dp', 'expert')), may hold values from -6 to 6
- expert_ids: int32 [4096, 2], P(('dp', 'expert')), may hold values from 0 to 3, all different within a row; in each aligned block of 128 rows (0 to 127, 128 to 255, ...) at most 96 rows name the same one
- routing: float32 [4096, 2], P(('dp', 'expert')), may hold values from 0.2 to 1
- w_gate: bfloat16 [4, 1024, 384], P('expert', 'dp'), may hold values from -0.1875 to 0.1875
- w_up: bfloat16 [4, 1024, 384], P('expert', 'dp'), may hold values from -0.1875 to 0.1875
- w_down: bfloat16 [4, 1024, 384], P('expert', 'dp'), may hold values from -0.3125 to 0.3125
- grad_out: bfloat16 [4096, 1024], P(('dp', 'expert')), may hold values from -6 to 6
Outputs:
- output: bfloat16 [4096, 1024], P(('dp', 'expert'))
- token_grad: bfloat16 [4096, 1024], P(('dp', 'expert'))
- down_grad: float32 [4, 1024, 384], P('expert', 'dp')
Inputs may be any that keep to these rules, and one draw needn't show every extreme that they name: `expert_ids`: the 2 experts of a token differ. Among the 128 tokens of one device no expert is named by more than 96 (token, choice) pairs, and in every draw some device names some expert exactly 96 times.
All inputs are finite; a program needn't handle non-finite values.
Results may differ from a plain program's by a relative error of at most 0.0065.
Values may be sent and summed in bfloat16 or wider, within the bound.
No kernel may reach another device: no remote copies, remote signals or barrier semaphores. Data moves between devices by JAX's collectives and lax.ppermute only.
A program may use at most 64 MiB of HBM per device.

v0:
```python
import jax
import jax.numpy as jnp
from jax import lax
from jax.sharding import PartitionSpec as P

contract_last = (((1,), (1,)), ((), ()))
contract_first = (((0,), (0,)), ((), ()))


def forward_rows(row_data, gate_w, up_w, down_w):
    gate_pre = jnp.dot(row_data, gate_w, preferred_element_type=jnp.float32)
    up_pre = jnp.dot(row_data, up_w, preferred_element_type=jnp.float32)
    sigmoid_val = jax.nn.sigmoid(gate_pre)
    hidden = (gate_pre * sigmoid_val * up_pre).astype(jnp.bfloat16)
    expert_out = lax.dot_general(
        hidden, down_w, contract_last, preferred_element_type=jnp.float32
    ).astype(jnp.bfloat16)
    return (gate_pre, up_pre, hidden, expert_out)


def backward_rows(grad_rows, gate_pre, up_pre, gate_w, up_w, down_w):
    hidden_grad = jnp.dot(grad_rows, down_w, preferred_element_type=jnp.float32)
    sigmoid_val = jax.nn.sigmoid(gate_pre)
    slope_val = sigmoid_val * (1.0 + gate_pre * (1.0 - sigmoid_val))
    gate_grad = (hidden_grad * up_pre * slope_val).astype(jnp.bfloat16)
    up_grad = (hidden_grad * gate_pre * sigmoid_val).astype(jnp.bfloat16)
    summed = lax.dot_general(gate_grad, gate_w, contract_last, preferred_element_type=jnp.float32)
    summed = summed + lax.dot_general(
        up_grad, up_w, contract_last, preferred_element_type=jnp.float32
    )
    return summed.astype(jnp.bfloat16)


def local(tokens, expert_ids, routing, w_gate, w_up, w_down, grad_out):
    tok_rows, width = tokens.shape
    groups = lax.axis_size("expert")
    local_count = w_gate.shape[0]
    ff_width = w_gate.shape[2]
    experts_all = local_count * groups
    top_count = expert_ids.shape[1]
    capacity = 3 * tok_rows * top_count // (2 * experts_all)
    pair_count = tok_rows * top_count
    chosen = expert_ids.reshape(pair_count)
    onehot = (chosen[:, None] == jnp.arange(experts_all, dtype=jnp.int32)[None, :]).astype(
        jnp.int32
    )
    before = jnp.cumsum(onehot, axis=0) - onehot
    slot_index = jnp.sum(before * onehot, axis=1)
    flat_index = chosen * capacity + slot_index
    owner_row = jnp.arange(pair_count, dtype=jnp.int32) // top_count
    slot_owner = (
        jnp.full((experts_all * capacity,), tok_rows, jnp.int32).at[flat_index].set(owner_row)
    )
    weight_slot = (
        jnp.zeros((experts_all * capacity,), jnp.float32)
        .at[flat_index]
        .set(routing.reshape(pair_count))
    )
    zero_row = jnp.zeros((1, width), jnp.bfloat16)
    send_rows = jnp.concatenate([tokens, zero_row], axis=0)[slot_owner].reshape(
        experts_all, capacity, width
    )
    grads_picked = jnp.concatenate([grad_out, zero_row], axis=0)[slot_owner].astype(jnp.float32)
    send_grads = (
        (weight_slot[:, None] * grads_picked)
        .astype(jnp.bfloat16)
        .reshape(experts_all, capacity, width)
    )
    shard_d = w_gate.shape[1]
    packed = jnp.concatenate([w_gate, w_up, w_down], axis=2)
    packed = jnp.transpose(packed, (1, 0, 2)).reshape(shard_d, local_count * 3 * ff_width)
    full = lax.all_gather(packed, "dp", axis=0, tiled=True)
    full = jnp.transpose(full.reshape(width, local_count, 3 * ff_width), (1, 0, 2))
    gate_full = full[:, :, :ff_width]
    up_full = full[:, :, ff_width : 2 * ff_width]
    down_full = full[:, :, 2 * ff_width :]
    recv_rows, recv_grads = (
        lax.all_to_all(send_rows, "expert", split_axis=0, concat_axis=0, tiled=True),
        lax.all_to_all(send_grads, "expert", split_axis=0, concat_axis=0, tiled=True),
    )
    rows_x = recv_rows.reshape(groups, local_count, capacity, width)
    rows_g = recv_grads.reshape(groups, local_count, capacity, width)
    slab_rows = groups * capacity
    expert_index = 0
    x_rows = rows_x[:, expert_index].reshape(slab_rows, width)
    g_rows = rows_g[:, expert_index].reshape(slab_rows, width)
    gate_w = gate_full[expert_index]
    up_w = up_full[expert_index]
    down_w = down_full[expert_index]
    is_valid = None
    position = None
    live_rows = None
    g_used = g_rows
    gate_pre, up_pre, hidden, expert_out = forward_rows(x_rows, gate_w, up_w, down_w)
    out_parts = [expert_out]
    forward_parts = [(gate_pre, up_pre, hidden, g_used, is_valid, position, live_rows)]
    out_send = jnp.stack(out_parts, axis=1).reshape(groups * local_count, capacity, width)
    back_out = lax.all_to_all(out_send, "expert", split_axis=0, concat_axis=0, tiled=True)
    expert_index = 0
    gate_pre, up_pre, hidden, g_used, is_valid, position, live_rows = forward_parts[expert_index]
    gate_w = gate_full[expert_index]
    up_w = up_full[expert_index]
    down_w = down_full[expert_index]
    grad_parts = [backward_rows(g_used, gate_pre, up_pre, gate_w, up_w, down_w)]
    grad_send = jnp.stack(grad_parts, axis=1).reshape(groups * local_count, capacity, width)
    back_grad = lax.all_to_all(grad_send, "expert", split_axis=0, concat_axis=0, tiled=True)
    out_rows = back_out.reshape(experts_all * capacity, width)[flat_index].reshape(
        tok_rows, top_count, width
    )
    output = jnp.sum(routing[:, :, None] * out_rows.astype(jnp.float32), axis=1).astype(
        jnp.bfloat16
    )
    grad_rows = back_grad.reshape(experts_all * capacity, width)[flat_index].reshape(
        tok_rows, top_count, width
    )
    token_grad = jnp.sum(grad_rows.astype(jnp.float32), axis=1).astype(jnp.bfloat16)
    shard_rows = w_gate.shape[1]
    saved = forward_parts[0]
    grad_cols = saved[3]
    pieces = lax.dot_general(
        grad_cols, saved[2], contract_first, preferred_element_type=jnp.float32
    )
    summed = lax.psum_scatter(pieces, "dp", scatter_dimension=0, tiled=True)
    down_grad = jnp.transpose(
        (summed / lax.axis_size("dp")).reshape(shard_rows, local_count, ff_width), (1, 0, 2)
    )
    return (output, token_grad, down_grad)


def solution(mesh):
    return jax.shard_map(
        local,
        mesh=mesh,
        in_specs=(
            P(("dp", "expert"), None),
            P(("dp", "expert"), None),
            P(("dp", "expert"), None),
            P("expert", "dp", None),
            P("expert", "dp", None),
            P("expert", "dp", None),
            P(("dp", "expert"), None),
        ),
        out_specs=(P(("dp", "expert"), None), P(("dp", "expert"), None), P("expert", "dp", None)),
        check_vma=False,
    )
```

profile of v0, /device:TPU:0, one launch (start us, length us, event | category | flops | bytes accessed | tf_op | source)
XLA Modules:
  0.0 127.7 jit_solution(5773724412011694440)
XLA Ops:
  7.2 0.0 all-gather.3.cloned.1.call-start
  7.2 1.7 %pad_maximum_fusion = bf16[1,128,1152]{2,1,0:T(8,128)(2,1)} fusion(bf16[1,128,384]{2,1,0:T(8,128)(2,1)} %param.12, bf16[1,128,384]{2,1,0:T(8,128)(2,1)} %param.11, bf16[1,128,384]{2,1,0:T(8,128)(2,1)} %param.10), kind=kLoop, calls=%fused_computation.22 | loop fusion | flops 884736 | bytes 589824 | tf_op jit(solution)/shard_map/concatenate | solution.py:70
  8.9 0.0 all-gather.3.cloned.1.call-update
  9.0 0.8 copy.15
  9.7 0.1 eq.29
  9.9 0.1 eq.25
  10.0 0.7 broadcast_multiply_fusion
  10.7 0.1 copy.14
  10.8 0.1 mul.65
  11.0 1.2 reduce-window.6
  12.2 0.1 slice.28
  12.3 0.1 copy.17
  12.4 0.1 copy.18
  12.5 1.0 concatenate.9
  13.5 0.1 add_bitcast_fusion
  13.6 1.4 %scatter_custom_fusion = s32[384]{0:T(512)S(1)} fusion(s32[256]{0:T(256)S(1)} %bitcast.61, s32[256]{0:T(256)S(1)} %and_select_fusion, s32[]{:T(128)} %constant.32.clone.1), kind=kCustom, calls=%fused_computation.43 | custom fusion | bytes 1540 | tf_op jit(solution)/shard_map/scatter | solution.py:52
  15.1 2.7 %gather_fusion = bf16[384,1024]{1,0:T(8,128)(2,1)} fusion(bf16[129,1024]{1,0:T(8,128)(2,1)S(1)} %concatenate.9, s32[1024]{0:T(1024)S(1)} %pad_clamp_fusion.1), kind=kCustom, calls=%fused_computation | custom fusion | bytes 1574400 | tf_op jit(solution)/shard_map/gather | solution.py:60
  17.8 6.3 %all-to-all-start = ((bf16[4,96,1024]{2,1,0:T(8,128)(2,1)}), bf16[4,96,1024]{2,1,0:T(8,128)(2,1)S(1)}, u32[]{:S(2)}, u32[]{:S(2)}) async-start(bf16[4,96,1024]{2,1,0:T(8,128)(2,1)} %bitcast.4), calls=%async_computation | async-start | bytes 1572864 | tf_op jit(solution)/shard_map/all_to_all | solution.py:78
  24.1 0.1 copy.13
  24.2 0.1 reshape.133
  24.4 1.4 %scatter_custom_fusion.1 = f32[384]{0:T(512)S(1)} fusion(s32[256]{0:T(256)S(1)} %bitcast.62, f32[256]{0:T(256)S(1)} %reshape.133, f32[]{:T(128)} %constant.40.clone.1), kind=kCustom, calls=%fused_computation.41 | custom fusion | bytes 1540 | tf_op jit(solution)/shard_map/scatter | solution.py:57
  25.8 0.1 mul.70
  25.9 2.1 %gather_fusion.2 = bf16[384,1024]{1,0:T(8,128)(2,1)S(1)} fusion(bf16[129,1024]{1,0:T(8,128)(2,1)S(1)} %concatenate.11, s32[1024]{0:T(1024)S(1)} %pad_clamp_fusion.1), kind=kCustom, calls=%fused_computation.2 | custom fusion | bytes 1574400 | tf_op jit(solution)/shard_map/gather | solution.py:63
  28.0 1.1 fusion
  29.0 15.2 %all-to-all-done = bf16[4,96,1024]{2,1,0:T(8,128)(2,1)S(1)} async-done(((bf16[4,96,1024]{2,1,0:T(8,128)(2,1)}), bf16[4,96,1024]{2,1,0:T(8,128)(2,1)S(1)}, u32[]{:S(2)}, u32[]{:S(2)}) %all-to-all-start) | async-done | bytes 786464 | tf_op jit(solution)/shard_map/all_to_all | solution.py:78
  44.2 3.5 %all-to-all-start.2 = ((bf16[4,96,1024]{2,1,0:T(8,128)(2,1)}), bf16[4,96,1024]{2,1,0:T(8,128)(2,1)S(1)}, u32[]{:S(2)}, u32[]{:S(2)}) async-start(bf16[4,96,1024]{2,1,0:T(8,128)(2,1)} %fusion), calls=%async_computation.2 | async-start | bytes 1572864 | tf_op jit(solution)/shard_map/all_to_all | solution.py:79
  47.7 0.0 all-gather.3.cloned.1.call-done
  47.7 1.7 %fusion.2 = f32[384,384]{1,0:T(8,128)S(1)} fusion(bf16[384,1024]{1,0:T(8,128)(2,1)S(1)} %bitcast.59, bf16[1,1024,1152]{2,1,0:T(8,128)(2,1)} %all-gather.3.cloned.1.call-done), kind=kOutput, calls=%fused_computation.15 | convolution fusion | flops 301989888 | bytes 2162688 | tf_op jit(solution)/shard_map/dot_general | solution.py:11
  49.4 1.7 %multiply_convert_fusion.2 = (bf16[384,384]{1,0:T(8,128)(2,1)S(1)}, f32[384,384]{1,0:T(8,128)S(1)}) fusion(f32[384,384]{1,0:T(8,128)S(1)} %fusion.2, bf16[384,1024]{1,0:T(8,128)(2,1)S(1)} %bitcast.60, bf16[1,1024,1152]{2,1,0:T(8,128)(2,1)} %all-gather.3.cloned.1.call-done), kind=kOutput, calls=%fused_computation.20 | convolution fusion | flops 302874624 | bytes 3047424 | tf_op jit(solution)/shard_map/dot_general | solution.py:12
  51.2 2.6 %convolution_convert_fusion = bf16[384,1024]{1,0:T(8,128)(2,1)} fusion(bf16[384,384]{1,0:T(8,128)(2,1)S(1)} %get-tuple-element.3, bf16[1,1024,1152]{2,1,0:T(8,128)(2,1)} %all-gather.3.cloned.1.call-done), kind=kOutput, calls=%fused_computation.9 | convolution fusion | flops 302383104 | bytes 1867776 | tf_op jit(solution)/shard_map/dot_general | solution.py:15
  53.8 13.6 %all-to-all-done.2 = bf16[4,96,1024]{2,1,0:T(8,128)(2,1)S(1)} async-done(((bf16[4,96,1024]{2,1,0:T(8,128)(2,1)}), bf16[4,96,1024]{2,1,0:T(8,128)(2,1)S(1)}, u32[]{:S(2)}, u32[]{:S(2)}) %all-to-all-start.2) | async-done | bytes 786464 | tf_op jit(solution)/shard_map/all_to_all | solution.py:79
  67.3 3.5 %all-to-all-start.1 = ((bf16[4,96,1024]{2,1,0:T(8,128)(2,1)}), bf16[4,96,1024]{2,1,0:T(8,128)(2,1)S(1)}, u32[]{:S(2)}, u32[]{:S(2)}) async-start(bf16[4,96,1024]{2,1,0:T(8,128)(2,1)} %bitcast.9), calls=%async_computation.1 | async-start | bytes 1572864 | tf_op jit(solution)/shard_map/all_to_all | solution.py:98
  70.8 0.0 reduce-scatter.2.cloned.1.call-start
  70.9 1.9 %fusion.16 = f32[1024,384]{1,0:T(8,128)} fusion(bf16[384,1024]{1,0:T(8,128)(2,1)S(1)} %bitcast.56, bf16[384,384]{1,0:T(8,128)(2,1)S(1)} %get-tuple-element.3), kind=kOutput, calls=%fused_computation.48 | convolution fusion | flops 301989888 | bytes 2654208 | tf_op jit(solution)/shard_map/dot_general | solution.py:120
  72.8 0.0 reduce-scatter.2.cloned.1.call-update
  72.8 1.7 %fusion.4 = f32[384,384]{1,0:T(8,128)S(1)} fusion(bf16[384,1024]{1,0:T(8,128)(2,1)S(1)} %bitcast.57, bf16[1,1024,1152]{2,1,0:T(8,128)(2,1)} %all-gather.3.cloned.1.call-done), kind=kOutput, calls=%fused_computation.17 | convolution fusion | flops 301989888 | bytes 2162688 | tf_op jit(solution)/shard_map/dot_general | solution.py:22
  74.5 1.8 %fusion.1 = f32[384,1024]{1,0:T(8,128)S(1)} fusion(bf16[1,1024,1152]{2,1,0:T(8,128)(2,1)} %all-gather.3.cloned.1.call-done, f32[384,384]{1,0:T(8,128)S(1)} %fusion.2, f32[384,384]{1,0:T(8,128)S(1)} %fusion.4, f32[384,384]{1,0:T(8,128)S(1)} %get-tuple-element.4), kind=kOutput, calls=%fused_computation.14 | convolution fusion | flops 303464448 | bytes 4128768 | tf_op jit(solution)/shard_map/dot_general | solution.py:27
  76.3 2.7 %add_convert_fusion = bf16[384,1024]{1,0:T(8,128)(2,1)} fusion(f32[384,1024]{1,0:T(8,128)S(1)} %fusion.1, bf16[1,1024,1152]{2,1,0:T(8,128)(2,1)} %all-gather.3.cloned.1.call-done, f32[384,384]{1,0:T(8,128)S(1)} %fusion.4, f32[384,384]{1,0:T(8,128)S(1)} %fusion.2), kind=kOutput, calls=%fused_computation.8 | convolution fusion | flops 303661056 | bytes 4325376 | tf_op jit(solution)/shard_map/dot_general | solution.py:28
  79.0 11.5 %all-to-all-done.1 = bf16[4,96,1024]{2,1,0:T(8,128)(2,1)S(1)} async-done(((bf16[4,96,1024]{2,1,0:T(8,128)(2,1)}), bf16[4,96,1024]{2,1,0:T(8,128)(2,1)S(1)}, u32[]{:S(2)}, u32[]{:S(2)}) %all-to-all-start.1) | async-done | bytes 786464 | tf_op jit(solution)/shard_map/all_to_all | solution.py:98
  90.5 3.7 %all-to-all-start.3 = ((bf16[4,96,1024]{2,1,0:T(8,128)(2,1)}), bf16[4,96,1024]{2,1,0:T(8,128)(2,1)S(1)}, u32[]{:S(2)}, u32[]{:S(2)}) async-start(bf16[4,96,1024]{2,1,0:T(8,128)(2,1)} %bitcast.13), calls=%async_computation.3 | async-start | bytes 1572864 | tf_op jit(solution)/shard_map/all_to_all | solution.py:106
  94.2 1.2 gather_fusion.1
  95.3 0.7 reshape.87
  96.0 17.6 %all-to-all-done.3 = bf16[4,96,1024]{2,1,0:T(8,128)(2,1)S(1)} async-done(((bf16[4,96,1024]{2,1,0:T(8,128)(2,1)}), bf16[4,96,1024]{2,1,0:T(8,128)(2,1)S(1)}, u32[]{:S(2)}, u32[]{:S(2)}) %all-to-all-start.3) | async-done | bytes 786464 | tf_op jit(solution)/shard_map/all_to_all | solution.py:106
  113.6 1.2 gather_fusion.3
  114.8 0.2 reshape.86
  115.0 2.1 %reduce_sum.35 = bf16[128,1024]{1,0:T(8,128)(2,1)} reduce(bf16[128,2,1024]{2,1,0:T(2,128)(2,1)S(1)} %reshape.86, bf16[]{:T(256)} %constant.16.clone.1), dimensions={1}, to_apply=%region_6.7 | reduce | flops 131072 | bytes 786434 | tf_op jit(solution)/shard_map/reduce_sum | solution.py:116
  117.1 2.1 %multiply_reduce_fusion = bf16[128,1024]{1,0:T(8,128)(2,1)} fusion(f32[128,2,1024]{2,1,0:T(2,128)S(1)} %reshape.87, f32[128,2]{1,0:T(8,128)S(1)} %copy.13), kind=kLoop, calls=%fused_computation.10 | loop fusion | flops 393216 | bytes 1311744 | tf_op jit(solution)/shard_map/reduce_sum | solution.py:110
  119.2 1.6 %multiply_bitcast_fusion = f32[1,128,384]{2,1,0:T(8,128)} fusion(f32[128,384]{1,0:T(8,128)} %reduce-scatter.2.cloned.1.call-done), kind=kLoop, calls=%fused_computation.25 | loop fusion | flops 49152 | bytes 393216 | tf_op jit(solution)/shard_map/transpose;reshape | solution.py:124
  (15 shorter events, 0.1 us)
Async XLA Ops:
  7.2 40.6 %all-gather.3.cloned.1.call-start = ((), (), s32[]{:S(2)}) async-start(), calls=%async_computation.6 | async-start | bytes 2654208 | tf_op jit(solution)/shard_map/all_gather | solution.py:72
  15.0 9.1 %copy-start.1 = (f32[128,2]{0,1:T(2,128)S(1)}, f32[128,2]{0,1:T(2,128)}, u32[]{:S(2)}) copy-start(f32[128,2]{0,1:T(2,128)} %param.9) | copy-start | bytes 3076
  15.1 10.8 %copy-start = (bf16[128,1024]{1,0:T(8,128)(2,1)S(1)}, bf16[128,1024]{1,0:T(8,128)(2,1)}, u32[]{:S(2)}) copy-start(bf16[128,1024]{1,0:T(8,128)(2,1)} %param.13) | copy-start | bytes 786436
  17.8 26.5 %all-to-all-start = ((bf16[4,96,1024]{2,1,0:T(8,128)(2,1)}), bf16[4,96,1024]{2,1,0:T(8,128)(2,1)S(1)}, u32[]{:S(2)}, u32[]{:S(2)}) async-start(bf16[4,96,1024]{2,1,0:T(8,128)(2,1)} %bitcast.4), calls=%async_computation | async-start | bytes 1572864 | tf_op jit(solution)/shard_map/all_to_all | solution.py:78
  44.2 23.1 %all-to-all-start.2 = ((bf16[4,96,1024]{2,1,0:T(8,128)(2,1)}), bf16[4,96,1024]{2,1,0:T(8,128)(2,1)S(1)}, u32[]{:S(2)}, u32[]{:S(2)}) async-start(bf16[4,96,1024]{2,1,0:T(8,128)(2,1)} %fusion), calls=%async_computation.2 | async-start | bytes 1572864 | tf_op jit(solution)/shard_map/all_to_all | solution.py:79
  67.3 23.1 %all-to-all-start.1 = ((bf16[4,96,1024]{2,1,0:T(8,128)(2,1)}), bf16[4,96,1024]{2,1,0:T(8,128)(2,1)S(1)}, u32[]{:S(2)}, u32[]{:S(2)}) async-start(bf16[4,96,1024]{2,1,0:T(8,128)(2,1)} %bitcast.9), calls=%async_computation.1 | async-start | bytes 1572864 | tf_op jit(solution)/shard_map/all_to_all | solution.py:98
  70.8 48.4 %reduce-scatter.2.cloned.1.call-start = ((), (), s32[]{:S(2)}) async-start(), calls=%async_computation.5 | async-start | bytes 1769472 | tf_op jit(solution)/shard_map/reduce_scatter | solution.py:123
  90.5 23.1 %all-to-all-start.3 = ((bf16[4,96,1024]{2,1,0:T(8,128)(2,1)}), bf16[4,96,1024]{2,1,0:T(8,128)(2,1)S(1)}, u32[]{:S(2)}, u32[]{:S(2)}) async-start(bf16[4,96,1024]{2,1,0:T(8,128)(2,1)} %bitcast.13), calls=%async_computation.3 | async-start | bytes 1572864 | tf_op jit(solution)/shard_map/all_to_all | solution.py:106
Sparse Core Ops, SparseCore 0:
  9.9 31.6 all-gather.2
  75.0 39.7 reduce-scatter.1
where the time goes:
time: 128 us
  waiting for transfers between devices  57.9 us (45%)
  starting transfers between devices  17.1 us (13%)
  between operations  14.2 us (11%)
  matrix products  14.1 us (11%)
  local copies, waits for them, and re-layouts  13.7 us (11%)
  other arithmetic  10.7 us (8%)
    all_to_all x1, waiting for transfers between devices, local(): lax.all_to_all(grad_send, 'expert', split_axis=0, concat_axis=0, tiled=True)  17.6 us
    all_to_all x1, waiting for transfers between devices, local(): lax.all_to_all(send_rows, 'expert', split_axis=0, concat_axis=0, tiled=True)  15.2 us
    all_to_all x1, waiting for transfers between devices, local(): lax.all_to_all(send_grads, 'expert', split_axis=0, concat_axis=0, tiled=T...  13.6 us
    all_to_all x1, waiting for transfers between devices, local(): lax.all_to_all(out_send, 'expert', split_axis=0, concat_axis=0, tiled=True)  11.5 us
    all_to_all x1, starting transfers between devices, local(): lax.all_to_all(send_rows, 'expert', split_axis=0, concat_axis=0, tiled=True)  6.35 us
    all_to_all x1, starting transfers between devices, local(): lax.all_to_all(grad_send, 'expert', split_axis=0, concat_axis=0, tiled=True)  3.67 us
    all_to_all x1, starting transfers between devices, local(): lax.all_to_all(send_grads, 'expert', split_axis=0, concat_axis=0, tiled=T...  3.49 us
    all_to_all x1, starting transfers between devices, local(): lax.all_to_all(out_send, 'expert', split_axis=0, concat_axis=0, tiled=True)  3.49 us
  transfers between devices with their start and end apart: 6, of which 4 were waited for; matrix products, arithmetic and copies ran while one was open for 27% of the time, Pallas kernels for 0%

commit v1 on v0

--- a/solution.py
+++ b/solution.py
@@ -5,6 +5,22 @@
 
 contract_last = (((1,), (1,)), ((), ()))
 contract_first = (((0,), (0,)), ((), ()))
+
+
+def swapped_with_each(value, axis, split, join):
+    ways, here = (lax.axis_size(axis), lax.axis_index(axis))
+    width = value.shape[split] // ways
+    shape = list(value.shape)
+    shape[split] = width
+    height = shape[join]
+    shape[join] = height * ways
+    full = jnp.zeros(shape, value.dtype)
+    for mask in range(ways):
+        part = lax.dynamic_slice_in_dim(value, (here ^ mask) * width, width, axis=split)
+        if mask:
+            part = lax.ppermute(part, axis, [(d, d ^ mask) for d in range(ways)])
+        full = lax.dynamic_update_slice_in_dim(full, part, (here ^ mask) * height, axis=join)
+    return full
 
 
 def forward_rows(row_data, gate_w, up_w, down_w):
@@ -103,7 +119,7 @@
     down_w = down_full[expert_index]
     grad_parts = [backward_rows(g_used, gate_pre, up_pre, gate_w, up_w, down_w)]
     grad_send = jnp.stack(grad_parts, axis=1).reshape(groups * local_count, capacity, width)
-    back_grad = lax.all_to_all(grad_send, "expert", split_axis=0, concat_axis=0, tiled=True)
+    back_grad = swapped_with_each(grad_send, "expert", 0, 0)
     out_rows = back_out.reshape(experts_all * capacity, width)[flat_index].reshape(
         tok_rows, top_count, width
     )

time: 128 us -> 126 us (0.984)
  waiting for transfers between devices: 57.9 us -> 54.4 us
    ppermute x0 -> x3, waiting for transfers between devices: none -> 23 us  [swapped_with_each(): part = lax.ppermute(part, axis, [(d, d ^ mask) for d in range(ways)])]
    all_to_all x1 -> x0, waiting for transfers between devices: 17.6 us -> none  [local(): lax.all_to_all(grad_send, 'expert', split_axis=0, concat_axis=0, tiled=True)]
    all_to_all x1, waiting for transfers between devices: 11.5 us -> 0.01 us  [local(): lax.all_to_all(out_send, 'expert', split_axis=0, concat_axis=0, tiled=True)]
    ppermute x0 -> x3, starting transfers between devices: none -> 4.45 us  [swapped_with_each(): part = lax.ppermute(part, axis, [(d, d ^ mask) for d in range(ways)])]
    all_to_all x1 -> x0, starting transfers between devices: 3.67 us -> none  [local(): lax.all_to_all(grad_send, 'expert', split_axis=0, concat_axis=0, tiled=True)]
    all_to_all x1, waiting for transfers between devices: 13.6 us -> 16.1 us  [local(): lax.all_to_all(send_grads, 'expert', split_axis=0, concat_axis=0, tiled=T...]
  transfers between devices with their start and end apart: 6 -> 8, of which waited for: 4 -> 4; matrix products, arithmetic and copies ran while one was open for 27% -> 26% of each run, Pallas kernels for 0% -> 0%
where the time goes in v1:
time: 126 us; the launch traced here: 125 us
  waiting for transfers between devices  54.4 us (43%)
  starting transfers between devices  18 us (14%)
  between operations  14.3 us (11%)
  local copies, waits for them, and re-layouts  13.9 us (11%)
  matrix products  13.3 us (11%)
  other arithmetic  10.7 us (8%)
    ppermute x3, waiting for transfers between devices, swapped_with_each(): part = lax.ppermute(part, axis, [(d, d ^ mask) for d in range(ways)])  23 us
    all_to_all x1, waiting for transfers between devices, local(): lax.all_to_all(send_grads, 'expert', split_axis=0, concat_axis=0, tiled=T...  16.1 us
    all_to_all x1, waiting for transfers between devices, local(): lax.all_to_all(send_rows, 'expert', split_axis=0, concat_axis=0, tiled=True)  15.1 us
    all_to_all x1, starting transfers between devices, local(): lax.all_to_all(send_rows, 'expert', split_axis=0, concat_axis=0, tiled=True)  6.35 us
    ppermute x3, starting transfers between devices, swapped_with_each(): part = lax.ppermute(part, axis, [(d, d ^ mask) for d in range(ways)])  4.45 us
    all_to_all x1, starting transfers between devices, local(): lax.all_to_all(out_send, 'expert', split_axis=0, concat_axis=0, tiled=True)  3.67 us
    all_to_all x1, starting transfers between devices, local(): lax.all_to_all(send_grads, 'expert', split_axis=0, concat_axis=0, tiled=T...  3.49 us
    gather x1, local copies, waits for them, and re-layouts, local(): jnp.concatenate([tokens, zero_row], axis=0)[slot_owner]  2.68 us
  transfers between devices with their start and end apart: 8, of which 4 were waited for; matrix products, arithmetic and copies ran while one was open for 26% of the time, Pallas kernels for 0%

profile of v1, /device:TPU:0, one launch (start us, length us, event | category | flops | bytes accessed | tf_op | source)
XLA Modules:
  0.0 124.6 jit_solution(18045329835678423451)
XLA Ops:
  7.2 1.7 %pad_maximum_fusion = bf16[1,128,1152]{2,1,0:T(8,128)(2,1)} fusion(bf16[1,128,384]{2,1,0:T(8,128)(2,1)} %param.12, bf16[1,128,384]{2,1,0:T(8,128)(2,1)} %param.11, bf16[1,128,384]{2,1,0:T(8,128)(2,1)} %param.10), kind=kLoop, calls=%fused_computation.22 | loop fusion | flops 884736 | bytes 589824 | tf_op jit(solution)/shard_map/concatenate | solution.py:86
  9.0 0.8 copy.15
  9.7 0.1 eq.29
  9.9 0.1 eq.25
  10.0 1.2 reduce-window.6
  11.3 0.1 slice.28
  11.3 0.1 copy.17
  11.5 0.1 copy.18
  11.6 0.7 broadcast_multiply_fusion
  12.3 0.1 copy.14
  12.4 0.1 mul.65
  12.5 1.0 concatenate.9
  13.5 0.1 add_bitcast_fusion
  13.6 1.4 %scatter_custom_fusion = s32[384]{0:T(512)S(1)} fusion(s32[256]{0:T(256)S(1)} %bitcast.60, s32[256]{0:T(256)S(1)} %and_select_fusion, s32[]{:T(128)} %constant.17.clone.1), kind=kCustom, calls=%fused_computation.50 | custom fusion | bytes 1540 | tf_op jit(solution)/shard_map/scatter | solution.py:68
  15.1 2.7 %gather_fusion = bf16[384,1024]{1,0:T(8,128)(2,1)} fusion(bf16[129,1024]{1,0:T(8,128)(2,1)S(1)} %concatenate.9, s32[1024]{0:T(1024)S(1)} %pad_clamp_fusion.1), kind=kCustom, calls=%fused_computation | custom fusion | bytes 1574400 | tf_op jit(solution)/shard_map/gather | solution.py:76
  17.7 6.3 %all-to-all-start = ((bf16[4,96,1024]{2,1,0:T(8,128)(2,1)}), bf16[4,96,1024]{2,1,0:T(8,128)(2,1)S(1)}, u32[]{:S(2)}, u32[]{:S(2)}) async-start(bf16[4,96,1024]{2,1,0:T(8,128)(2,1)} %bitcast.4), calls=%async_computation | async-start | bytes 1572864 | tf_op jit(solution)/shard_map/all_to_all | solution.py:94
  24.1 2.1 %gather_fusion.2 = bf16[384,1024]{1,0:T(8,128)(2,1)S(1)} fusion(bf16[129,1024]{1,0:T(8,128)(2,1)S(1)} %concatenate.11, s32[1024]{0:T(1024)S(1)} %pad_clamp_fusion.1), kind=kCustom, calls=%fused_computation.2 | custom fusion | bytes 1574400 | tf_op jit(solution)/shard_map/gather | solution.py:79
  26.2 0.1 copy.13
  26.3 0.1 reshape.133
  26.5 1.4 %scatter_custom_fusion.1 = f32[384]{0:T(512)S(1)} fusion(s32[256]{0:T(256)S(1)} %bitcast.61, f32[256]{0:T(256)S(1)} %reshape.133, f32[]{:T(128)} %constant.47.clone.1), kind=kCustom, calls=%fused_computation.48 | custom fusion | bytes 1540 | tf_op jit(solution)/shard_map/scatter | solution.py:73
  27.9 0.1 mul.70
  28.0 1.1 fusion
  29.1 15.1 %all-to-all-done = bf16[4,96,1024]{2,1,0:T(8,128)(2,1)S(1)} async-done(((bf16[4,96,1024]{2,1,0:T(8,128)(2,1)}), bf16[4,96,1024]{2,1,0:T(8,128)(2,1)S(1)}, u32[]{:S(2)}, u32[]{:S(2)}) %all-to-all-start) | async-done | bytes 786464 | tf_op jit(solution)/shard_map/all_to_all | solution.py:94
  44.2 3.5 %all-to-all-start.2 = ((bf16[4,96,1024]{2,1,0:T(8,128)(2,1)}), bf16[4,96,1024]{2,1,0:T(8,128)(2,1)S(1)}, u32[]{:S(2)}, u32[]{:S(2)}) async-start(bf16[4,96,1024]{2,1,0:T(8,128)(2,1)} %fusion), calls=%async_computation.2 | async-start | bytes 1572864 | tf_op jit(solution)/shard_map/all_to_all | solution.py:95
  47.7 0.0 reduce-scatter.2.cloned.1.call-start
  47.8 1.7 %fusion.2 = f32[384,384]{1,0:T(8,128)S(1)} fusion(bf16[384,1024]{1,0:T(8,128)(2,1)S(1)} %bitcast.57, bf16[1,1024,1152]{2,1,0:T(8,128)(2,1)} %all-gather.3.cloned.1.call-done), kind=kOutput, calls=%fused_computation.15 | convolution fusion | flops 301989888 | bytes 2162688 | tf_op jit(solution)/shard_map/dot_general | solution.py:27
  49.5 1.7 %multiply_convert_fusion.2 = (bf16[384,384]{1,0:T(8,128)(2,1)S(1)}, f32[384,384]{1,0:T(8,128)S(1)}) fusion(f32[384,384]{1,0:T(8,128)S(1)} %fusion.2, bf16[384,1024]{1,0:T(8,128)(2,1)S(1)} %bitcast.58, bf16[1,1024,1152]{2,1,0:T(8,128)(2,1)} %all-gather.3.cloned.1.call-done), kind=kOutput, calls=%fused_computation.20 | convolution fusion | flops 302874624 | bytes 3047424 | tf_op jit(solution)/shard_map/dot_general | solution.py:28
  51.2 16.1 %all-to-all-done.2 = bf16[4,96,1024]{2,1,0:T(8,128)(2,1)S(1)} async-done(((bf16[4,96,1024]{2,1,0:T(8,128)(2,1)}), bf16[4,96,1024]{2,1,0:T(8,128)(2,1)S(1)}, u32[]{:S(2)}, u32[]{:S(2)}) %all-to-all-start.2) | async-done | bytes 786464 | tf_op jit(solution)/shard_map/all_to_all | solution.py:95
  67.3 1.9 %fusion.16 = f32[1024,384]{1,0:T(8,128)} fusion(bf16[384,1024]{1,0:T(8,128)(2,1)S(1)} %bitcast.54, bf16[384,384]{1,0:T(8,128)(2,1)S(1)} %get-tuple-element.7), kind=kOutput, calls=%fused_computation.55 | convolution fusion | flops 301989888 | bytes 2654208 | tf_op jit(solution)/shard_map/dot_general | solution.py:136
  69.2 2.6 %convolution_convert_fusion = bf16[384,1024]{1,0:T(8,128)(2,1)} fusion(bf16[384,384]{1,0:T(8,128)(2,1)S(1)} %get-tuple-element.7, bf16[1,1024,1152]{2,1,0:T(8,128)(2,1)} %all-gather.3.cloned.1.call-done), kind=kOutput, calls=%fused_computation.9 | convolution fusion | flops 302383104 | bytes 1867776 | tf_op jit(solution)/shard_map/dot_general | solution.py:31
  71.8 3.7 %all-to-all-start.1 = ((bf16[4,96,1024]{2,1,0:T(8,128)(2,1)}), bf16[4,96,1024]{2,1,0:T(8,128)(2,1)S(1)}, u32[]{:S(2)}, u32[]{:S(2)}) async-start(bf16[4,96,1024]{2,1,0:T(8,128)(2,1)} %bitcast.9), calls=%async_computation.1 | async-start | bytes 1572864 | tf_op jit(solution)/shard_map/all_to_all | solution.py:114
  75.5 1.7 %fusion.4 = f32[384,384]{1,0:T(8,128)S(1)} fusion(bf16[384,1024]{1,0:T(8,128)(2,1)S(1)} %bitcast.55, bf16[1,1024,1152]{2,1,0:T(8,128)(2,1)} %all-gather.3.cloned.1.call-done), kind=kOutput, calls=%fused_computation.17 | convolution fusion | flops 301989888 | bytes 2162688 | tf_op jit(solution)/shard_map/dot_general | solution.py:38
  77.3 1.8 %fusion.1 = f32[384,1024]{1,0:T(8,128)S(1)} fusion(bf16[1,1024,1152]{2,1,0:T(8,128)(2,1)} %all-gather.3.cloned.1.call-done, f32[384,384]{1,0:T(8,128)S(1)} %fusion.2, f32[384,384]{1,0:T(8,128)S(1)} %fusion.4, f32[384,384]{1,0:T(8,128)S(1)} %get-tuple-element.8), kind=kOutput, calls=%fused_computation.14 | convolution fusion | flops 303464448 | bytes 4128768 | tf_op jit(solution)/shard_map/dot_general | solution.py:43
  79.1 1.8 %add_convert_fusion = bf16[384,1024]{1,0:T(8,128)(2,1)S(1)} fusion(f32[384,1024]{1,0:T(8,128)S(1)} %fusion.1, bf16[1,1024,1152]{2,1,0:T(8,128)(2,1)} %all-gather.3.cloned.1.call-done, f32[384,384]{1,0:T(8,128)S(1)} %fusion.4, f32[384,384]{1,0:T(8,128)S(1)} %fusion.2), kind=kOutput, calls=%fused_computation.8 | convolution fusion | flops 303661056 | bytes 4325376 | tf_op jit(solution)/shard_map/dot_general | solution.py:44
  80.9 0.1 broadcast_in_dim.10
  81.0 0.1 constant_dynamic-slice_fusion.2
  81.1 1.9 %collective-permute-start = (bf16[1,96,1024]{2,1,0:T(8,128)(2,1)S(1)}, bf16[1,96,1024]{2,1,0:T(8,128)(2,1)S(1)}, u32[]{:S(2)}, u32[]{:S(2)}) collective-permute-start(bf16[1,96,1024]{2,1,0:T(8,128)(2,1)S(1)} %get-tuple-element.5), channel_id=1, source_target_pairs={{0,1},{1,0},{2,3},{3,2},{4,5},{5,4},{6,7},{7,6},{8,9},{9,8},{10,11... | collective-permute-start | bytes 589832 | tf_op jit(solution)/shard_map/ppermute | solution.py:21
  83.0 2.4 %collective-permute-start.1 = (bf16[1,96,1024]{2,1,0:T(8,128)(2,1)S(1)}, bf16[1,96,1024]{2,1,0:T(8,128)(2,1)S(1)}, u32[]{:S(2)}, u32[]{:S(2)}) collective-permute-start(bf16[1,96,1024]{2,1,0:T(8,128)(2,1)S(1)} %get-tuple-element.4), channel_id=1, source_target_pairs={{0,2},{1,3},{2,0},{3,1},{4,6},{5,7},{6,4},{7,5},{8,10},{9,11},{10,... | collective-permute-start | bytes 589832 | tf_op jit(solution)/shard_map/ppermute | solution.py:21
  85.4 0.2 collective-permute-start.2
  85.6 8.1 %collective-permute-done = bf16[1,96,1024]{2,1,0:T(8,128)(2,1)S(1)} collective-permute-done((bf16[1,96,1024]{2,1,0:T(8,128)(2,1)S(1)}, bf16[1,96,1024]{2,1,0:T(8,128)(2,1)S(1)}, u32[]{:S(2)}, u32[]{:S(2)}) %collective-permute-start) | collective-permute-done | bytes 196640 | tf_op jit(solution)/shard_map/ppermute | solution.py:21
  93.7 14.9 %collective-permute-done.1 = bf16[1,96,1024]{2,1,0:T(8,128)(2,1)S(1)} collective-permute-done((bf16[1,96,1024]{2,1,0:T(8,128)(2,1)S(1)}, bf16[1,96,1024]{2,1,0:T(8,128)(2,1)S(1)}, u32[]{:S(2)}, u32[]{:S(2)}) %collective-permute-start.1) | collective-permute-done | bytes 196640 | tf_op jit(solution)/shard_map/ppermute | solution.py:21
  108.7 1.2 gather_fusion.3
  109.8 0.2 reshape.86
  110.1 2.1 %reduce_sum.35 = bf16[128,1024]{1,0:T(8,128)(2,1)} reduce(bf16[128,2,1024]{2,1,0:T(2,128)(2,1)S(1)} %reshape.86, bf16[]{:T(256)} %constant.16.clone.1), dimensions={1}, to_apply=%region_6.7 | reduce | flops 131072 | bytes 786434 | tf_op jit(solution)/shard_map/reduce_sum | solution.py:132
  112.2 1.2 gather_fusion.1
  113.4 0.7 reshape.87
  114.0 2.1 %multiply_reduce_fusion = bf16[128,1024]{1,0:T(8,128)(2,1)} fusion(f32[128,2,1024]{2,1,0:T(2,128)S(1)} %reshape.87, f32[128,2]{1,0:T(8,128)S(1)} %copy.13), kind=kLoop, calls=%fused_computation.10 | loop fusion | flops 393216 | bytes 1311744 | tf_op jit(solution)/shard_map/reduce_sum | solution.py:126
  116.1 1.6 %multiply_bitcast_fusion = f32[1,128,384]{2,1,0:T(8,128)} fusion(f32[128,384]{1,0:T(8,128)} %reduce-scatter.2.cloned.1.call-done), kind=kLoop, calls=%fused_computation.26 | loop fusion | flops 49152 | bytes 393216 | tf_op jit(solution)/shard_map/transpose;reshape | solution.py:140
  (24 shorter events, 0.3 us)
Async XLA Ops:
  7.2 40.6 %all-gather.3.cloned.1.call-start = ((), (), s32[]{:S(2)}) async-start(), calls=%async_computation.5 | async-start | bytes 2654208 | tf_op jit(solution)/shard_map/all_gather | solution.py:88
  15.0 9.0 %copy-start = (bf16[128,1024]{1,0:T(8,128)(2,1)S(1)}, bf16[128,1024]{1,0:T(8,128)(2,1)}, u32[]{:S(2)}) copy-start(bf16[128,1024]{1,0:T(8,128)(2,1)} %param.13) | copy-start | bytes 786436
  17.7 26.5 %all-to-all-start = ((bf16[4,96,1024]{2,1,0:T(8,128)(2,1)}), bf16[4,96,1024]{2,1,0:T(8,128)(2,1)S(1)}, u32[]{:S(2)}, u32[]{:S(2)}) async-start(bf16[4,96,1024]{2,1,0:T(8,128)(2,1)} %bitcast.4), calls=%async_computation | async-start | bytes 1572864 | tf_op jit(solution)/shard_map/all_to_all | solution.py:94
  24.1 2.1 %copy-start.1 = (f32[128,2]{0,1:T(2,128)S(1)}, f32[128,2]{0,1:T(2,128)}, u32[]{:S(2)}) copy-start(f32[128,2]{0,1:T(2,128)} %param.9) | copy-start | bytes 3076
  44.2 23.1 %all-to-all-start.2 = ((bf16[4,96,1024]{2,1,0:T(8,128)(2,1)}), bf16[4,96,1024]{2,1,0:T(8,128)(2,1)S(1)}, u32[]{:S(2)}, u32[]{:S(2)}) async-start(bf16[4,96,1024]{2,1,0:T(8,128)(2,1)} %fusion), calls=%async_computation.2 | async-start | bytes 1572864 | tf_op jit(solution)/shard_map/all_to_all | solution.py:95
  47.7 68.4 %reduce-scatter.2.cloned.1.call-start = ((), (), s32[]{:S(2)}) async-start(), calls=%async_computation.4 | async-start | bytes 1769472 | tf_op jit(solution)/shard_map/reduce_scatter | solution.py:139
  71.8 40.4 %all-to-all-start.1 = ((bf16[4,96,1024]{2,1,0:T(8,128)(2,1)}), bf16[4,96,1024]{2,1,0:T(8,128)(2,1)S(1)}, u32[]{:S(2)}, u32[]{:S(2)}) async-start(bf16[4,96,1024]{2,1,0:T(8,128)(2,1)} %bitcast.9), calls=%async_computation.1 | async-start | bytes 1572864 | tf_op jit(solution)/shard_map/all_to_all | solution.py:114
  81.1 12.6 %collective-permute-start = (bf16[1,96,1024]{2,1,0:T(8,128)(2,1)S(1)}, bf16[1,96,1024]{2,1,0:T(8,128)(2,1)S(1)}, u32[]{:S(2)}, u32[]{:S(2)}) collective-permute-start(bf16[1,96,1024]{2,1,0:T(8,128)(2,1)S(1)} %get-tuple-element.5), channel_id=1, source_target_pairs={{0,1},{1,0},{2,3},{3,2},{4,5},{5,4},{6,7},{7,6},{8,9},{9,8},{10,11... | collective-permute-start | bytes 589832 | tf_op jit(solution)/shard_map/ppermute | solution.py:21
  83.0 25.6 %collective-permute-start.1 = (bf16[1,96,1024]{2,1,0:T(8,128)(2,1)S(1)}, bf16[1,96,1024]{2,1,0:T(8,128)(2,1)S(1)}, u32[]{:S(2)}, u32[]{:S(2)}) collective-permute-start(bf16[1,96,1024]{2,1,0:T(8,128)(2,1)S(1)} %get-tuple-element.4), channel_id=1, source_target_pairs={{0,2},{1,3},{2,0},{3,1},{4,6},{5,7},{6,4},{7,5},{8,10},{9,11},{10,... | collective-permute-start | bytes 589832 | tf_op jit(solution)/shard_map/ppermute | solution.py:21
  85.4 23.3 %collective-permute-start.2 = (bf16[1,96,1024]{2,1,0:T(8,128)(2,1)S(1)}, bf16[1,96,1024]{2,1,0:T(8,128)(2,1)S(1)}, u32[]{:S(2)}, u32[]{:S(2)}) collective-permute-start(bf16[1,96,1024]{2,1,0:T(8,128)(2,1)S(1)} %get-tuple-element.3), channel_id=1, source_target_pairs={{0,3},{1,2},{2,1},{3,0},{4,7},{5,6},{6,5},{7,4},{8,11},{9,10},{10,... | collective-permute-start | bytes 589832 | tf_op jit(solution)/shard_map/ppermute | solution.py:21
Sparse Core Ops, SparseCore 0:
  9.9 31.5 all-gather.2
  69.3 37.4 reduce-scatter.1
